TPU v7x, 32 devices: a whole 2x2x4 slice. The times are simulated.
32 devices in a mesh: layer: 4 (over y, x), tok: 8 (over z, core).
Axes of the slice: x: 2, y: 2, z: 4, core: 2. Of those that a mesh axis runs over, the one named last changes fastest.
Arguments:
- residual: bfloat16 [4, 1024, 3584], P('layer', 'tok'), may hold values from -6 to 6
- targets: bfloat16 [4, 1024, 3584], P('layer', 'tok'), may hold values from -6 to 6
- block_ids: int32 [4, 1024, 2], P(None, 'tok'), may hold values from 0 to 127, all different within a row; in each aligned block of 128 rows (0 to 127, 128 to 255, ..., all dimensions but the last counted through in order) at most 4 rows name the same one
- encoder_weight: bfloat16 [4, 3584, 16384], P('layer', None, 'tok'), may hold values from -0.09375 to 0.09375
- encoder_bias: float32 [4, 16384], P('layer', 'tok'), may hold values from -3 to 3
- decoder_weight: bfloat16 [4, 4, 16384, 3584], P('layer', None, 'tok'), may hold values from -0.25 to 0.25
- decoder_bias: float32 [4, 3584], P('layer'), may hold values from -3 to 3
Outputs:
- reconstruction: bfloat16 [4, 1024, 3584], P('layer', 'tok')
- error: float32 [4, 1024], P('layer', 'tok')
Inputs may be any that keep to these rules, and one draw needn't show every extreme that they name: `block_ids`: A token's 2 blocks in a layer are distinct. In each layer, the 128 rows of one device (aligned blocks of tokens) name no block more than 4 times, and some block exactly 4 times.
All inputs are finite; a program needn't handle non-finite values.
Results may differ from a plain program's by a relative error of at most 0.0053.
Values may be sent and summed in bfloat16 or wider, within the bound.
No kernel may reach another device: no remote copies, remote signals or barrier semaphores. Data moves between devices by JAX's collectives and lax.ppermute only.
A program may use at most 192 MiB of HBM per device.

v0:
```python
import jax
import jax.numpy as jnp
from jax import lax
from jax.sharding import PartitionSpec as P

BLOCK = 128


def slot_positions(ids, blocks, capacity):
    flat_ids = ids.reshape(-1)
    onehot = (flat_ids[:, None] == jnp.arange(blocks, dtype=jnp.int32)[None, :]).astype(jnp.int32)
    before = jnp.cumsum(onehot, axis=0) - onehot
    rank_in = jnp.sum(before * onehot, axis=1)
    return flat_ids * capacity + rank_in


def body(residual, targets, block_ids, encoder_weight, encoder_bias, decoder_weight, decoder_bias):
    layer_index = lax.axis_index("layer")
    layers = lax.axis_size("layer")
    tok_count = lax.axis_size("tok")
    tok_rows = residual.shape[1]
    width = residual.shape[2]
    topk = block_ids.shape[2]
    per_owner = encoder_weight.shape[2] // BLOCK
    blocks = per_owner * tok_count
    capacity = max(2, 2 * tok_rows * topk // blocks)
    slot_count = blocks * capacity
    positions = jax.vmap(lambda ids: slot_positions(ids, blocks, capacity))(block_ids)
    own_positions = lax.dynamic_index_in_dim(positions, layer_index, 0, keepdims=False)
    source_row = (
        jnp.full((slot_count,), tok_rows, jnp.int32)
        .at[own_positions]
        .set(jnp.arange(tok_rows * topk, dtype=jnp.int32) // topk)
    )
    padded = jnp.concatenate([residual[0], jnp.zeros((1, width), residual.dtype)], axis=0)
    outgoing = padded[source_row].reshape(tok_count, per_owner * capacity, width)
    arrived = lax.all_to_all(outgoing, "tok", split_axis=0, concat_axis=0, tiled=True)
    arrived = arrived.reshape(tok_count, per_owner, capacity, width)
    enc_blocks = encoder_weight[0].reshape(width, per_owner, BLOCK)
    pre = jnp.einsum("sbcd,dbe->sbce", arrived, enc_blocks, preferred_element_type=jnp.float32)
    pre = pre + encoder_bias[0].reshape(per_owner, BLOCK)[None, :, None, :]
    codes = (
        jnp.maximum(pre, 0.0)
        .astype(jnp.bfloat16)
        .reshape(1, tok_count, per_owner * capacity, BLOCK)
    )
    all_codes = lax.all_gather(codes, "layer", axis=0, tiled=True)
    sources = jnp.arange(layers, dtype=jnp.int32)
    valid = sources <= layer_index
    weights = decoder_weight[0]
    keep_slot = valid.astype(jnp.float32)
    slot_sets = sources.shape[0]
    chosen_codes = (
        jnp.take(all_codes, sources, axis=0) * valid.astype(jnp.bfloat16)[:, None, None, None]
    )
    terms = (
        jnp.einsum(
            "snbce,sbed->snbcd",
            chosen_codes.reshape(slot_sets, tok_count, per_owner, capacity, BLOCK),
            weights.reshape(slot_sets, per_owner, BLOCK, width),
            preferred_element_type=jnp.float32,
        )
        .astype(jnp.bfloat16)
        .reshape(slot_sets, tok_count, per_owner * capacity, width)
    )
    returned = lax.all_to_all(terms, "tok", split_axis=1, concat_axis=1, tiled=True).reshape(
        slot_sets, slot_count, width
    )
    source_positions = jnp.take(positions, sources, axis=0)
    picked = jax.vmap(lambda rows, where_at: rows[where_at])(returned, source_positions)
    parts = jnp.sum(picked.astype(jnp.float32).reshape(slot_sets, tok_rows, topk, width), axis=2)
    own_sum = jnp.sum(parts * keep_slot[:, None, None], axis=0)
    recon32 = decoder_bias[0][None, :] + own_sum
    difference = recon32 - targets[0].astype(jnp.float32)
    error = jnp.mean(difference * difference, axis=1)
    return (recon32.astype(jnp.bfloat16)[None], error[None])


def solution(mesh):
    in_specs = (
        P("layer", "tok", None),
        P("layer", "tok", None),
        P(None, "tok", None),
        P("layer", None, "tok"),
        P("layer", "tok"),
        P("layer", None, "tok", None),
        P("layer", None),
    )
    out_specs = (P("layer", "tok", None), P("layer", "tok"))
    return jax.shard_map(body, mesh=mesh, in_specs=in_specs, out_specs=out_specs, check_vma=False)
```

profile of v0, /device:TPU:0, one launch (start us, length us, event | category | flops | bytes accessed | tf_op | source)
XLA Modules:
  0.0 584.5 jit_solution(2805510803366540468)
XLA Ops:
  0.6 0.8 copy.34
  1.5 1.0 copy.38
  2.5 0.9 fusion.14
  3.4 0.2 broadcast_add_fusion
  3.7 0.1 copy.35
  3.8 0.4 fusion.16
  4.2 1.4 scatter_custom_fusion
  5.6 1.2 concatenate.3
  6.9 4.2 gather_fusion
  11.1 6.3 %all-to-all-start = ((bf16[8,64,3584]{2,1,0:T(8,128)(2,1)}), bf16[8,64,3584]{2,1,0:T(8,128)(2,1)}, u32[]{:S(2)}, u32[]{:S(2)}) async-start(bf16[8,64,3584]{2,1,0:T(8,128)(2,1)} %bitcast.60), calls=%async_computation | async-start | bytes 7340032 | tf_op jit(solution)/shard_map/all_to_all | solution.py:37
  17.4 14.5 %copy.50 = bf16[448,8,16,128]{3,2,1,0:T(8,128)(2,1)} copy(bf16[448,8,16,128]{3,1,2,0:T(8,128)(2,1)} %bitcast.61) | data formatting | bytes 29360128
  31.9 0.0 copy-start.2
  31.9 68.3 %all-to-all-done = bf16[8,64,3584]{2,1,0:T(8,128)(2,1)} async-done(((bf16[8,64,3584]{2,1,0:T(8,128)(2,1)}), bf16[8,64,3584]{2,1,0:T(8,128)(2,1)}, u32[]{:S(2)}, u32[]{:S(2)}) %all-to-all-start) | async-done | bytes 3670048 | tf_op jit(solution)/shard_map/all_to_all | solution.py:37
  100.3 4.1 copy.40
  104.3 0.0 copy-done.2
  104.3 13.2 %fusion.11 = bf16[16,8,4,128]{3,1,2,0:T(8,128)(2,1)S(1)} fusion(bf16[8,16,4,3584]{3,0,2,1:T(8,128)(2,1)S(1)} %bitcast.63, bf16[3584,16,128,1]{2,1,0,3:T(8,128)(2,1)} %bitcast.62, f32[16,128]{1,0:T(8,128)S(1)} %bitcast.70), kind=kOutput, calls=%fused_computation.16 | convolution fusion | flops 469958656 | bytes 18489344 | tf_op jit(solution)/shard_map/sbcd,dbe->sbce/dot_general | solution.py:40
  117.6 10.2 %all_gather.3 = bf16[4,8,64,128]{3,2,1,0:T(8,128)(2,1)S(1)} all-gather(bf16[1,8,64,128]{3,2,1,0:T(8,128)(2,1)S(1)} %copy.42), channel_id=1, replica_groups=mesh['layer'=4,'tok'=8] {'layer'}, dimensions={0}, use_global_device_ids=true | all-gather | bytes 655360 | tf_op jit(solution)/shard_map/all_gather | solution.py:47
  127.8 0.6 gather_fusion.1
  128.5 25.9 %convolution_convert_fusion = bf16[4,16,8,4,3584]{4,2,3,1,0:T(8,128)(2,1)} fusion(bf16[4,16,128,3584,1]{3,2,4,1,0:T(8,128)(2,1)} %bitcast.59, bf16[4,8,16,4,128]{4,3,2,1,0:T(4,128)(2,1)S(1)} %bitcast.64, pred[4]{0:T(512)(128)(4,1)S(1)} %get-tuple-element.3, bf16[4]{0:T(256)(128)(2,1)S(1)} %get-tuple-element.2), kind=kOutput, calls=%fused_computation.7 | convolution fusion | flops 1886912512 | bytes 73924624 | tf_op jit(solution)/shard_map/snbce,sbed->snbcd/dot_general | solution.py:57
  154.4 15.6 %copy.44 = bf16[4,8,64,3584]{3,2,0,1:T(8,128)(2,1)} copy(bf16[4,8,64,3584]{3,1,2,0:T(8,128)(2,1)} %bitcast.58) | data formatting | bytes 29360128 | tf_op jit(solution)/shard_map/reshape | solution.py:64
  170.0 0.0 copy-start.1
  170.0 5.7 all-to-all-start.1
  175.7 0.6 gather_fusion.2
  176.2 0.1 fusion.27
  176.3 0.0 copy-done.1
  176.4 318.0 %all-to-all-done.1 = bf16[4,8,64,3584]{3,2,0,1:T(8,128)(2,1)} async-done(((bf16[4,8,64,3584]{3,2,0,1:T(8,128)(2,1)}), bf16[4,8,64,3584]{3,2,0,1:T(8,128)(2,1)}, u32[]{:S(2)}, u32[]{:S(2)}) %all-to-all-start.1) | async-done | bytes 14680096 | tf_op jit(solution)/shard_map/all_to_all | solution.py:66
  494.4 13.4 %copy.45 = bf16[4,8,64,3584]{3,2,1,0:T(8,128)(2,1)} copy(bf16[4,8,64,3584]{3,2,0,1:T(8,128)(2,1)} %all-to-all-done.1) | data formatting | bytes 29360128 | tf_op jit(solution)/shard_map/all_to_all | solution.py:66
  507.8 32.0 %gather_fusion.3 = bf16[1024,3584]{1,0:T(8,128)(2,1)} fusion(bf16[4,512,3584]{2,1,0:T(8,128)(2,1)} %bitcast.56, s32[1024]{0:T(1024)S(1)} %bitcast.57), kind=kCustom, calls=%fused_computation.3 | custom fusion | bytes 14688256 | tf_op jit(solution)/shard_map/vmap()/gather | solution.py:70
  539.8 16.2 %reshape.172 = f32[4,128,2,3584]{3,2,1,0:T(2,128)} reshape(bf16[1024,3584]{1,0:T(8,128)(2,1)} %gather_fusion.3) | data formatting | bytes 22020096 | tf_op jit(solution)/shard_map/convert_element_type | solution.py:71
  556.0 22.3 %reduce_sum.39 = f32[4,128,3584]{2,1,0:T(8,128)} reduce(f32[4,128,2,3584]{3,2,1,0:T(2,128)} %reshape.172, f32[]{:T(128)} %constant.75.clone.1), dimensions={2}, to_apply=%region_4.5 | reduce | flops 1835008 | bytes 22020100 | tf_op jit(solution)/shard_map/reduce_sum | solution.py:71
  578.3 0.0 copy-start
  578.3 4.3 multiply_reduce_fusion
  582.6 1.0 fusion.4
  583.6 0.0 copy-done
  583.6 0.4 fusion.3
  584.0 0.5 multiply_bitcast_fusion
  (16 shorter events, 0.2 us)
Async XLA Ops:
  11.1 89.2 %all-to-all-start = ((bf16[8,64,3584]{2,1,0:T(8,128)(2,1)}), bf16[8,64,3584]{2,1,0:T(8,128)(2,1)}, u32[]{:S(2)}, u32[]{:S(2)}) async-start(bf16[8,64,3584]{2,1,0:T(8,128)(2,1)} %bitcast.60), calls=%async_computation | async-start | bytes 7340032 | tf_op jit(solution)/shard_map/all_to_all | solution.py:37
  31.9 72.4 %copy-start.2 = (f32[1,2048]{1,0:T(1,128)S(1)}, f32[1,2048]{1,0:T(1,128)}, u32[]{:S(2)}) copy-start(f32[1,2048]{1,0:T(1,128)} %param.11) | copy-start | bytes 24580
  170.0 6.3 %copy-start.1 = (f32[1,3584]{1,0:T(1,128)S(1)}, f32[1,3584]{1,0:T(1,128)}, u32[]{:S(2)}) copy-start(f32[1,3584]{1,0:T(1,128)} %param.13) | copy-start | bytes 43012
  170.0 324.4 %all-to-all-start.1 = ((bf16[4,8,64,3584]{3,2,0,1:T(8,128)(2,1)}), bf16[4,8,64,3584]{3,2,0,1:T(8,128)(2,1)}, u32[]{:S(2)}, u32[]{:S(2)}) async-start(bf16[4,8,64,3584]{3,2,0,1:T(8,128)(2,1)} %copy.44), calls=%async_computation.1 | async-start | bytes 29360128 | tf_op jit(solution)/shard_map/all_to_all | solution.py:66
  578.3 5.3 copy-start
where the time goes:
time: 586 us; the launch traced here: 585 us
  waiting for transfers between devices  386 us (66%)
  local copies, waits for them, and re-layouts  106 us (18%)
  matrix products  39.1 us (7%)
  other arithmetic  30.2 us (5%)
  starting transfers between devices  12 us (2%)
  blocking collectives  10.2 us (2%)
    all_to_all x1, waiting for transfers between devices, body(): lax.all_to_all(terms, 'tok', split_axis=1, concat_axis=1, tiled=True)  318 us
    all_to_all x1, waiting for transfers between devices, body(): lax.all_to_all(outgoing, 'tok', split_axis=0, concat_axis=0, tiled=True)  68.3 us
    gather x1, local copies, waits for them, and re-layouts, body(): rows[where_at]  32 us
    dot_general x1, matrix products, body(): jnp.einsum('snbce,sbed->snbcd', chosen_codes.reshape(slot_sets, tok_count...  25.9 us
    reduce_sum x1, other arithmetic, body(): jnp.sum(picked.astype(jnp.float32).reshape(slot_sets, tok_rows, topk, wid...  22.3 us
    convert_element_type x1, local copies, waits for them, and re-layouts, body(): picked.astype(jnp.float32).reshape(slot_sets, tok_rows, topk, width)  16.2 us
    reshape x1, local copies, waits for them, and re-layouts, body(): terms = jnp.einsum('snbce,sbed->snbcd', chosen_codes.reshape(slot_sets, t...  15.6 us
    unnamed x9, local copies, waits for them, and re-layouts  15.3 us
  transfers between devices with their start and end apart: 2, of which 2 were waited for; matrix products, arithmetic and copies ran while one was open for 3% of the time, Pallas kernels for 0%

commit v1 on v0

--- a/solution.py
+++ b/solution.py
@@ -4,6 +4,15 @@
 from jax.sharding import PartitionSpec as P
 
 BLOCK = 128
+check_inputs_on_mesh = lambda x0: jnp.concatenate(
+    lax.all_to_all(
+        jnp.stack(jnp.split(x0, lax.axis_size("tok"), 1), 0),
+        axis_name="tok",
+        split_axis=0,
+        concat_axis=0,
+    ),
+    1,
+)
 
 
 def slot_positions(ids, blocks, capacity):
@@ -63,9 +72,7 @@
         .astype(jnp.bfloat16)
         .reshape(slot_sets, tok_count, per_owner * capacity, width)
     )
-    returned = lax.all_to_all(terms, "tok", split_axis=1, concat_axis=1, tiled=True).reshape(
-        slot_sets, slot_count, width
-    )
+    returned = check_inputs_on_mesh(terms).reshape(slot_sets, slot_count, width)
     source_positions = jnp.take(positions, sources, axis=0)
     picked = jax.vmap(lambda rows, where_at: rows[where_at])(returned, source_positions)
     parts = jnp.sum(picked.astype(jnp.float32).reshape(slot_sets, tok_rows, topk, width), axis=2)

time: 586 us -> 635 us (1.084)
  local copies, waits for them, and re-layouts: 106 us -> 155 us
    split x0 -> x1, local copies, waits for them, and re-layouts: none -> 48.9 us  [jnp.split(x0, lax.axis_size('tok'), 1)]
    unnamed x9 -> x28, local copies, waits for them, and re-layouts: 15.3 us -> 30.6 us
    all_to_all x1 -> x0, local copies, waits for them, and re-layouts: 13.4 us -> none  [body(): lax.all_to_all(terms, 'tok', split_axis=1, concat_axis=1, tiled=True)]
  transfers between devices with their start and end apart: 2 -> 2, of which waited for: 2 -> 2; matrix products, arithmetic and copies ran while one was open for 3% -> 2% of each run, Pallas kernels for 0% -> 0%
where the time goes in v1:
time: 635 us; the launch traced here: 633 us
  waiting for transfers between devices  386 us (61%)
  local copies, waits for them, and re-layouts  155 us (24%)
  matrix products  39.2 us (6%)
  other arithmetic  30.2 us (5%)
  starting transfers between devices  12.2 us (2%)
  blocking collectives  10.2 us (2%)
    all_to_all x1, waiting for transfers between devices, lax.all_to_all(jnp.stack(jnp.split(x0, lax.axis_size('tok'), 1), 0), axis...  318 us
    all_to_all x1, waiting for transfers between devices, body(): lax.all_to_all(outgoing, 'tok', split_axis=0, concat_axis=0, tiled=True)  68.3 us
    split x1, local copies, waits for them, and re-layouts, jnp.split(x0, lax.axis_size('tok'), 1)  48.9 us
    gather x1, local copies, waits for them, and re-layouts, body(): rows[where_at]  31.9 us
    unnamed x28, local copies, waits for them, and re-layouts  30.6 us
    dot_general x1, matrix products, body(): jnp.einsum('snbce,sbed->snbcd', chosen_codes.reshape(slot_sets, tok_count...  25.9 us
    reduce_sum x1, other arithmetic, body(): jnp.sum(picked.astype(jnp.float32).reshape(slot_sets, tok_rows, topk, wid...  22.3 us
    convert_element_type x1, local copies, waits for them, and re-layouts, body(): picked.astype(jnp.float32).reshape(slot_sets, tok_rows, topk, width)  16.2 us
  transfers between devices with their start and end apart: 2, of which 2 were waited for; matrix products, arithmetic and copies ran while one was open for 2% of the time, Pallas kernels for 0%

profile of v1, /device:TPU:0, one launch (start us, length us, event | category | flops | bytes accessed | tf_op | source)
XLA Modules:
  0.0 633.4 jit_solution(7401362681930557928)
XLA Ops:
  0.6 0.0 copy-start.5
  0.7 0.9 copy.56
  1.6 1.0 copy.60
  2.6 0.9 fusion.22
  3.5 0.2 broadcast_add_fusion
  3.8 0.1 copy.57
  3.8 0.4 fusion.24
  4.3 1.4 scatter_custom_fusion
  5.7 0.0 copy-done.5
  5.7 0.1 concatenate.3
  5.8 4.2 gather_fusion
  10.0 6.3 all-to-all-start
  16.3 14.5 %copy.87 = bf16[448,8,16,128]{3,2,1,0:T(8,128)(2,1)} copy(bf16[448,8,16,128]{3,1,2,0:T(8,128)(2,1)} %bitcast.94) | data formatting | bytes 29360128
  30.8 0.0 copy-start.8
  30.9 68.3 %all-to-all-done = bf16[8,64,3584]{2,1,0:T(8,128)(2,1)} async-done(((bf16[8,64,3584]{2,1,0:T(8,128)(2,1)}), bf16[8,64,3584]{2,1,0:T(8,128)(2,1)}, u32[]{:S(2)}, u32[]{:S(2)}) %all-to-all-start) | async-done | bytes 3670048 | tf_op jit(solution)/shard_map/all_to_all | solution.py:46
  99.2 4.1 copy.62
  103.3 0.0 copy-done.8
  103.3 13.2 %fusion.19 = bf16[16,8,4,128]{3,1,2,0:T(8,128)(2,1)S(1)} fusion(bf16[8,16,4,3584]{3,0,2,1:T(8,128)(2,1)S(1)} %bitcast.96, bf16[3584,16,128,1]{2,1,0,3:T(8,128)(2,1)} %bitcast.95, f32[16,128]{1,0:T(8,128)S(1)} %bitcast.103), kind=kOutput, calls=%fused_computation.32 | convolution fusion | flops 469958656 | bytes 18489344 | tf_op jit(solution)/shard_map/sbcd,dbe->sbce/dot_general | solution.py:49
  116.5 10.2 %all_gather.3 = bf16[4,8,64,128]{3,2,1,0:T(8,128)(2,1)S(1)} all-gather(bf16[1,8,64,128]{3,2,1,0:T(8,128)(2,1)S(1)} %copy.64), channel_id=1, replica_groups=mesh['layer'=4,'tok'=8] {'layer'}, dimensions={0}, use_global_device_ids=true | all-gather | bytes 655360 | tf_op jit(solution)/shard_map/all_gather | solution.py:56
  126.7 0.6 gather_fusion.1
  127.4 25.9 %convolution_convert_fusion = bf16[4,16,8,4,3584]{4,2,3,1,0:T(8,128)(2,1)} fusion(bf16[4,16,128,3584,1]{3,2,4,1,0:T(8,128)(2,1)} %bitcast.92, bf16[4,8,16,4,128]{4,3,2,1,0:T(4,128)(2,1)S(1)} %bitcast.97, pred[4]{0:T(512)(128)(4,1)S(1)} %get-tuple-element.11, bf16[4]{0:T(256)(128)(2,1)S(1)} %get-tuple-element.10), kind=kOutput, calls=%fused_computation.7 | convolution fusion | flops 1886912512 | bytes 73924624 | tf_op jit(solution)/shard_map/snbce,sbed->snbcd/dot_general | solution.py:66
  153.3 48.9 %fusion.39 = (bf16[4,1,64,3584]{3,1,2,0:T(2,128)(2,1)S(1)}, bf16[4,1,64,3584]{3,1,2,0:T(2,128)(2,1)S(1)}, bf16[4,1,64,3584]{3,1,2,0:T(2,128)(2,1)}, bf16[4,1,64,...) fusion(bf16[4,8,64,3584]{3,1,2,0:T(8,128)(2,1)} %bitcast.90), kind=kLoop, calls=%fused_computation.70 | loop fusion | bytes 29360128 | tf_op jit(solution)/shard_map/split | solution.py:9
  202.3 0.0 copy-start.4
  202.3 3.7 fusion.9
  206.0 0.0 copy-start.3
  206.0 0.0 copy-done.4
  206.0 1.5 fusion.8
  207.4 0.0 copy-start.2
  207.4 1.2 copy-done.3
  208.7 1.5 fusion.7
  210.2 0.0 copy-start.1
  210.2 0.0 copy-done.2
  210.2 1.5 fusion.6
  211.7 0.0 copy-start
  211.7 1.2 copy-done.1
  212.9 1.6 fusion.5
  214.4 0.0 copy-done
  214.4 1.5 fusion.4
  215.9 1.5 fusion.3
  217.4 1.5 fusion.2
  218.9 0.0 copy-start.7
  218.9 5.9 all-to-all-start.1
  224.8 0.6 gather_fusion.2
  225.4 0.1 fusion.35
  225.5 0.0 copy-done.7
  225.5 317.8 %all-to-all-done.1 = bf16[8,4,1,64,3584]{4,3,1,2,0:T(8,128)(2,1)} async-done(((bf16[8,4,1,64,3584]{4,3,1,2,0:T(8,128)(2,1)}), bf16[8,4,1,64,3584]{4,3,1,2,0:T(8,128)(2,1)}, u32[]{:S(2)}, u32[]{:S(2)}) %all-to-all-start.1) | async-done | bytes 14680096 | tf_op jit(solution)/shard_map/all_to_all | solution.py:8
  543.3 13.5 %copy.74 = bf16[4,8,1,64,3584]{4,3,1,0,2:T(8,128)(2,1)} copy(bf16[4,8,1,64,3584]{4,3,0,2,1:T(8,128)(2,1)} %bitcast.29) | data formatting | bytes 29360128 | tf_op jit(solution)/shard_map/reshape | solution.py:7
  556.8 31.9 %gather_fusion.3 = bf16[1024,3584]{1,0:T(8,128)(2,1)} fusion(bf16[4,512,3584]{2,1,0:T(8,128)(2,1)} %bitcast.89, s32[1024]{0:T(1024)S(1)} %bitcast.91), kind=kCustom, calls=%fused_computation.3 | custom fusion | bytes 14688256 | tf_op jit(solution)/shard_map/vmap()/gather | solution.py:77
  588.7 16.2 %reshape.172 = f32[4,128,2,3584]{3,2,1,0:T(2,128)} reshape(bf16[1024,3584]{1,0:T(8,128)(2,1)} %gather_fusion.3) | data formatting | bytes 22020096 | tf_op jit(solution)/shard_map/convert_element_type | solution.py:78
  604.8 22.3 %reduce_sum.39 = f32[4,128,3584]{2,1,0:T(8,128)} reduce(f32[4,128,2,3584]{3,2,1,0:T(2,128)} %reshape.172, f32[]{:T(128)} %constant.75.clone.1), dimensions={2}, to_apply=%region_4.5 | reduce | flops 1835008 | bytes 22020100 | tf_op jit(solution)/shard_map/reduce_sum | solution.py:78
  627.2 0.0 copy-start.6
  627.2 4.3 multiply_reduce_fusion
  631.4 1.0 fusion.12
  632.5 0.0 copy-done.6
  632.5 0.4 fusion.11
  632.9 0.5 multiply_bitcast_fusion
  (16 shorter events, 0.2 us)
Async XLA Ops:
  0.6 5.1 copy-start.5
  10.0 89.2 %all-to-all-start = ((bf16[8,64,3584]{2,1,0:T(8,128)(2,1)}), bf16[8,64,3584]{2,1,0:T(8,128)(2,1)}, u32[]{:S(2)}, u32[]{:S(2)}) async-start(bf16[8,64,3584]{2,1,0:T(8,128)(2,1)} %bitcast.93), calls=%async_computation | async-start | bytes 7340032 | tf_op jit(solution)/shard_map/all_to_all | solution.py:46
  30.8 72.4 %copy-start.8 = (f32[1,2048]{1,0:T(1,128)S(1)}, f32[1,2048]{1,0:T(1,128)}, u32[]{:S(2)}) copy-start(f32[1,2048]{1,0:T(1,128)} %param.11) | copy-start | bytes 24580
  202.3 3.7 copy-start.4
  206.0 2.7 copy-start.3
  207.4 2.7 copy-start.2
  210.2 2.7 copy-start.1
  211.7 2.7 copy-start
  218.9 6.6 %copy-start.7 = (f32[1,3584]{1,0:T(1,128)S(1)}, f32[1,3584]{1,0:T(1,128)}, u32[]{:S(2)}) copy-start(f32[1,3584]{1,0:T(1,128)} %param.13) | copy-start | bytes 43012
  218.9 324.4 %all-to-all-start.1 = ((bf16[8,4,1,64,3584]{4,3,1,2,0:T(8,128)(2,1)}), bf16[8,4,1,64,3584]{4,3,1,2,0:T(8,128)(2,1)}, u32[]{:S(2)}, u32[]{:S(2)}) async-start(bf16[8,4,1,64,3584]{4,3,1,2,0:T(8,128)(2,1)} %fusion.2), calls=%async_computation.1 | async-start | bytes 29360128 | tf_op jit(solution)/shard_map/all_to_all | solution.py:8
  627.2 5.3 copy-start.6
